TPU v7x, 256 devices: a whole 4x4x8 slice. The times are simulated.
256 devices in a mesh: seq: 32 (over y, x, z_lo), tp: 8 (over z_hi, core).
Axes of the slice: x: 4, y: 4, z: 8 (z_hi: 4, z_lo: 2; z = z_hi * 2 + z_lo), core: 2. Of those that a mesh axis runs over, the one named last changes fastest.
Arguments:
- tokens: bfloat16 [32768, 2048], P('seq'), may hold values from -20 to 20
- w_query: bfloat16 [2048, 2048], P(None, 'tp'), may hold values from -0.15467961 to 0.15467961
- w_kv: bfloat16 [2048, 512], replicated, may hold values from -0.110485435 to 0.110485435
- w_out: bfloat16 [2048, 2048], P('tp'), may hold values from -6 to 6
- seg_start: int32 [32768], P('seq'), may hold values from 0 to 32752, as said below
- page_owner: int32 [2048], replicated, may hold values from 0 to 31, as said below
- page_slot: int32 [2048], replicated, may hold values from 0 to 127, as said below
Outputs:
- layer_out: bfloat16 [32768, 2048], P('seq', 'tp')
- kv_cache: bfloat16 [65536, 512], P('seq', 'tp')
Inputs may be any that keep to these rules, and one draw needn't show every extreme that they name: seg_start[t] is the first position of the prompt that holds token t: it never falls along the stream, is a multiple of 16, is at most t, and equals t at each prompt's first token; the last page begins a prompt. `page_owner`: among the 64 pages of one stream block no owner is named more than 4 times; one owner is named exactly 4 times by the pages of every block. `page_slot`: pages with the same owner have distinct slots.
All inputs are finite; a program needn't handle non-finite values.
Results may differ from a plain program's by a relative error of at most 0.015.
Values may be sent and summed in bfloat16 or wider, within the bound.
No kernel may reach another device: no remote copies, remote signals or barrier semaphores. Data moves between devices by JAX's collectives and lax.ppermute only.
A program may use at most 64 MiB of HBM per device.

v0:
```python
import jax
import jax.numpy as jnp
from jax import lax
from jax.sharding import PartitionSpec as P

H = 32
KVH = 4
HD = 64
WINDOW = 2048
PAGE = 16
masked_value = -1e30


def passed_along(value, axis, steps):
    count = lax.axis_size(axis)
    leading, last = (max(0, -steps), min(count, count - steps))
    return lax.ppermute(value, axis, [(source, source + steps) for source in range(leading, last)])


def attend_band(query_block, band_block, positions_q, positions_k, starts):
    keys_block = band_block[:, :, 0, :]
    values_block = band_block[:, :, 1, :]
    head_size = query_block.shape[-1]
    scores = jnp.einsum(
        "qkgd,ckd->kgqc", query_block, keys_block, preferred_element_type=jnp.float32
    ) * head_size ** (-0.5)
    lower_bound = jnp.maximum(starts, positions_q - WINDOW + 1)
    visible = (positions_k[None, :] >= lower_bound[:, None]) & (
        positions_k[None, :] <= positions_q[:, None]
    )
    scores = jnp.where(visible, scores, masked_value)
    largest = jnp.max(scores, axis=-1, keepdims=True)
    powered = jnp.exp(scores - largest)
    row_total = jnp.sum(powered, axis=-1, keepdims=True)
    weights = powered.astype(jnp.bfloat16)
    result = (
        jnp.einsum("kgqc,ckd->kgqd", weights, values_block, preferred_element_type=jnp.float32)
        / row_total
    )
    return jnp.transpose(result, (2, 0, 1, 3)).astype(jnp.bfloat16)


def body(tokens, w_query, w_kv, w_out, seg_start, page_owner, page_slot):
    seq_index = lax.axis_index("seq")
    tp_index = lax.axis_index("tp")
    seq_count = lax.axis_size("seq")
    tp_count = lax.axis_size("tp")
    tok_rows = tokens.shape[0]
    group_size = H // KVH
    heads_dev = H // tp_count
    kv_heads_dev = max(1, heads_dev // group_size)
    kv_width = kv_heads_dev * 2 * HD
    cache_width = KVH * 2 * HD // tp_count
    first_col = tp_index * heads_dev // group_size * 2 * HD
    queries = jnp.dot(tokens, w_query, preferred_element_type=jnp.float32).astype(jnp.bfloat16)
    w_local = lax.dynamic_slice_in_dim(w_kv, first_col, kv_width, 1)
    key_value = jnp.dot(tokens, w_local, preferred_element_type=jnp.float32).astype(jnp.bfloat16)
    own_cols = lax.dynamic_slice_in_dim(
        key_value, tp_index * cache_width - first_col, cache_width, 1
    )
    pages_dev = tok_rows // PAGE
    slots_per = max(2, 2 * pages_dev // seq_count)
    cache_slots = seq_count * slots_per
    owners_all = page_owner.reshape(seq_count, pages_dev)
    owner_hot = (
        owners_all[:, :, None] == jnp.arange(seq_count, dtype=jnp.int32)[None, None, :]
    ).astype(jnp.int32)
    local_rank = jnp.sum((jnp.cumsum(owner_hot, axis=1) - owner_hot) * owner_hot, axis=2)
    column_of = jnp.arange(seq_count, dtype=jnp.int32)[:, None] * slots_per + local_rank
    own_owner = lax.dynamic_index_in_dim(owners_all, seq_index, 0, keepdims=False)
    own_rank = lax.dynamic_index_in_dim(local_rank, seq_index, 0, keepdims=False)
    destination = own_owner * slots_per + own_rank
    send_table = (jnp.arange(cache_slots, dtype=jnp.int32)[:, None] == destination[None, :]).astype(
        jnp.bfloat16
    )
    page_rows = own_cols.reshape(pages_dev, PAGE * cache_width)
    outgoing_pages = jnp.dot(send_table, page_rows, preferred_element_type=jnp.float32).astype(
        jnp.bfloat16
    )
    outgoing_pages = outgoing_pages.reshape(seq_count, slots_per, PAGE * cache_width)
    arrived = lax.all_to_all(outgoing_pages, "seq", split_axis=0, concat_axis=0, tiled=True)
    owned_here = page_owner == seq_index
    place_table = (
        (page_slot[None, :] == jnp.arange(cache_slots, dtype=jnp.int32)[:, None])
        & owned_here[None, :]
    ).astype(jnp.bfloat16)
    pick_table = (
        column_of.reshape(-1)[:, None] == jnp.arange(cache_slots, dtype=jnp.int32)[None, :]
    ).astype(jnp.bfloat16)
    route_table = jnp.dot(place_table, pick_table, preferred_element_type=jnp.float32).astype(
        jnp.bfloat16
    )
    cache_local = jnp.dot(
        route_table,
        arrived.reshape(cache_slots, PAGE * cache_width),
        preferred_element_type=jnp.float32,
    )
    kv_cache = cache_local.astype(jnp.bfloat16).reshape(cache_slots * PAGE, cache_width)
    blocks_back = WINDOW // tok_rows
    pieces = []
    for distance in range(blocks_back, 0, -1):
        pieces.append(passed_along(key_value, "seq", distance))
    behind = jnp.concatenate(pieces, axis=0)
    band_all = jnp.concatenate([behind, key_value], axis=0).reshape(-1, kv_heads_dev, 2, HD)
    query_heads = queries.reshape(tok_rows, kv_heads_dev, heads_dev // kv_heads_dev, HD)
    block_rows = min(256, tok_rows)
    base_position = seq_index * tok_rows

    def one_block(block_idx):
        first_row = block_idx * block_rows
        query_block = lax.dynamic_slice_in_dim(query_heads, first_row, block_rows, 0)
        band_block = lax.dynamic_slice_in_dim(band_all, first_row, WINDOW + block_rows, 0)
        starts = lax.dynamic_slice_in_dim(seg_start, first_row, block_rows, 0)
        positions_q = base_position + first_row + jnp.arange(block_rows, dtype=jnp.int32)
        positions_k = (
            base_position + first_row - WINDOW + jnp.arange(WINDOW + block_rows, dtype=jnp.int32)
        )
        return attend_band(query_block, band_block, positions_q, positions_k, starts)

    attended = lax.map(one_block, jnp.arange(tok_rows // block_rows, dtype=jnp.int32))
    attended = attended.reshape(tok_rows, heads_dev * HD)
    projected = jnp.dot(attended, w_out, preferred_element_type=jnp.float32)
    summed = lax.psum(projected.astype(jnp.bfloat16), "tp").astype(jnp.float32)
    width_dev = summed.shape[1] // tp_count
    layer_out = lax.dynamic_slice_in_dim(summed, tp_index * width_dev, width_dev, 1).astype(
        jnp.bfloat16
    )
    return (layer_out, kv_cache)


def solution(mesh):
    return jax.shard_map(
        body,
        mesh=mesh,
        in_specs=(P("seq", None), P(None, "tp"), P(), P("tp", None), P("seq"), P(), P()),
        out_specs=(P("seq", "tp"), P("seq", "tp")),
        check_vma=False,
    )
```

profile of v0, /device:TPU:65, one launch (start us, length us, event | category | flops | bytes accessed | tf_op | source)
XLA Modules:
  0.0 213.9 jit_solution(16457602136221309663)
XLA Ops:
  7.2 1.5 copy-done
  8.8 3.7 %convolution_convert_fusion.4 = bf16[128,1024]{1,0:T(8,128)(2,1)S(1)} fusion(bf16[1024,2048]{1,0:T(8,128)(2,1)} %param.9, bf16[2048,512]{1,0:T(8,128)(2,1)S(1)} %copy-done, s32[]{:T(128)S(6)} %select_n.52), kind=kOutput, calls=%fused_computation.32 | convolution fusion | flops 537001984 | bytes 4980740 | tf_op jit(solution)/shard_map/dot_general | solution.py:57
  12.5 3.6 %collective-permute-start.1 = (bf16[1024,128]{0,1:T(8,128)(2,1)S(1)}, bf16[1024,128]{0,1:T(8,128)(2,1)S(1)}, u32[]{:S(2)}, u32[]{:S(2)}) collective-permute-start(bf16[1024,128]{0,1:T(8,128)(2,1)S(1)} %bitcast.95), channel_id=1, source_target_pairs={{0,8},{8,16},{16,24},{24,32},{32,40},{40,48},{48,56},{56,64},{64,7... | collective-permute-start | bytes 786440 | tf_op jit(solution)/shard_map/ppermute | solution.py:17
  16.1 3.1 %collective-permute-start = (bf16[1024,128]{0,1:T(8,128)(2,1)S(1)}, bf16[1024,128]{0,1:T(8,128)(2,1)S(1)}, u32[]{:S(2)}, u32[]{:S(2)}) collective-permute-start(bf16[1024,128]{0,1:T(8,128)(2,1)S(1)} %bitcast.96), channel_id=1, source_target_pairs={{0,16},{8,24},{16,32},{24,40},{32,48},{40,56},{48,64},{56,72},{64,... | collective-permute-start | bytes 786440 | tf_op jit(solution)/shard_map/ppermute | solution.py:17
  19.2 4.6 %convolution_convert_fusion.1 = bf16[1024,256]{0,1:T(8,128)(2,1)} fusion(bf16[1024,2048]{1,0:T(8,128)(2,1)} %param.9, bf16[2048,256]{1,0:T(8,128)(2,1)} %param.10), kind=kOutput, calls=%fused_computation.29 | convolution fusion | flops 1074003968 | bytes 5767168 | tf_op jit(solution)/shard_map/dot_general | solution.py:55
  23.8 4.3 %collective-permute-done = bf16[1024,128]{0,1:T(8,128)(2,1)S(1)} collective-permute-done((bf16[1024,128]{0,1:T(8,128)(2,1)S(1)}, bf16[1024,128]{0,1:T(8,128)(2,1)S(1)}, u32[]{:S(2)}, u32[]{:S(2)}) %collective-permute-start) | collective-permute-done | bytes 262176 | tf_op jit(solution)/shard_map/ppermute | solution.py:17
  28.1 0.9 pad_maximum_fusion
  29.1 47.1 %while.15 = (s32[]{:T(128)}, bf16[4,256,1,4,64]{1,4,3,2,0:T(8,128)(2,1)}, s32[4]{0:T(128)S(1)}, s32[]{:T(128)}, s32[1024]{0:T(1024)}, /*index=5*/bf16[3072,1,2,6...) while((s32[]{:T(128)}, ...), condition=%wide.region_3.4_spmd, body=%wide.region_0.0_spmd.sunk | while | flops 631833600 | bytes 31567140 | solution.py:120
  29.1 0.6 dynamic_slice.80
  30.3 0.8 add_maximum_fusion.2
  31.1 1.1 compare_and_fusion.2
  32.2 2.6 %fusion.55 = (f32[4,256]{1,0:T(4,128)S(1)}, f32[2304,256,4]{1,0,2:T(8,128)S(1)}) fusion(pred[256,2304]{0,1:T(8,128)(4,1)S(1)} %compare_and_fusion.2, bf16[1024,1,4,64]{0,3,2,1:T(8,128)(2,1)} %get-tuple-element.277, s32[]{:T(128)S(6)} %select_n.82, bf16[3072,1,2,64]{0,3,2,1:T(8,128)(2,1)} %get-tuple-element.276, s32[]{:T(128)S(6)} %select_n.83), kind=kOutput, calls=%fused_computation.4.clone.1 | convolution fusion | flops 309066752 | bytes 10457096 | tf_op jit(solution)/shard_map/while/body/eval_jaxpr/qkgd,ckd->kgqc/dot_general | solution.py:24
  34.8 2.0 fusion.56
  36.8 4.1 %fusion.57 = bf16[4,256,1,4,64]{1,4,3,2,0:T(8,128)(2,1)} fusion(bf16[4,256,1,4,64]{1,4,3,2,0:T(8,128)(2,1)} %get-tuple-element.258, s32[]{:T(128)S(6)} %copy.40, f32[2304,256,4]{1,0,2:T(8,128)S(1)} %get-tuple-element.241, f32[4,256]{1,0:T(4,128)S(1)} %get-tuple-element.242, pred[256,2304]{0,1:T(8,128)(4,1)S(1)} %compare_and_fusion.2, ...), kind=kOutput, calls=%fused_computation.12.clone.1 | convolution fusion | flops 311558144 | bytes 10461196 | tf_op jit(solution)/shard_map/while/body/eval_jaxpr/kgqc,ckd->kgqd/dot_general | solution.py:37
  40.8 0.6 dynamic_slice.80
  42.1 0.8 add_maximum_fusion.2
  42.9 1.1 compare_and_fusion.2
  43.9 2.6 %fusion.55 = (f32[4,256]{1,0:T(4,128)S(1)}, f32[2304,256,4]{1,0,2:T(8,128)S(1)}) fusion(pred[256,2304]{0,1:T(8,128)(4,1)S(1)} %compare_and_fusion.2, bf16[1024,1,4,64]{0,3,2,1:T(8,128)(2,1)} %get-tuple-element.277, s32[]{:T(128)S(6)} %select_n.82, bf16[3072,1,2,64]{0,3,2,1:T(8,128)(2,1)} %get-tuple-element.276, s32[]{:T(128)S(6)} %select_n.83), kind=kOutput, calls=%fused_computation.4.clone.1 | convolution fusion | flops 309066752 | bytes 10457096 | tf_op jit(solution)/shard_map/while/body/eval_jaxpr/qkgd,ckd->kgqc/dot_general | solution.py:24
  46.6 2.0 fusion.56
  48.6 4.1 %fusion.57 = bf16[4,256,1,4,64]{1,4,3,2,0:T(8,128)(2,1)} fusion(bf16[4,256,1,4,64]{1,4,3,2,0:T(8,128)(2,1)} %get-tuple-element.258, s32[]{:T(128)S(6)} %copy.40, f32[2304,256,4]{1,0,2:T(8,128)S(1)} %get-tuple-element.241, f32[4,256]{1,0:T(4,128)S(1)} %get-tuple-element.242, pred[256,2304]{0,1:T(8,128)(4,1)S(1)} %compare_and_fusion.2, ...), kind=kOutput, calls=%fused_computation.12.clone.1 | convolution fusion | flops 311558144 | bytes 10461196 | tf_op jit(solution)/shard_map/while/body/eval_jaxpr/kgqc,ckd->kgqd/dot_general | solution.py:37
  52.6 0.6 dynamic_slice.80
  53.9 0.8 add_maximum_fusion.2
  54.6 1.1 compare_and_fusion.2
  55.7 2.6 %fusion.55 = (f32[4,256]{1,0:T(4,128)S(1)}, f32[2304,256,4]{1,0,2:T(8,128)S(1)}) fusion(pred[256,2304]{0,1:T(8,128)(4,1)S(1)} %compare_and_fusion.2, bf16[1024,1,4,64]{0,3,2,1:T(8,128)(2,1)} %get-tuple-element.277, s32[]{:T(128)S(6)} %select_n.82, bf16[3072,1,2,64]{0,3,2,1:T(8,128)(2,1)} %get-tuple-element.276, s32[]{:T(128)S(6)} %select_n.83), kind=kOutput, calls=%fused_computation.4.clone.1 | convolution fusion | flops 309066752 | bytes 10457096 | tf_op jit(solution)/shard_map/while/body/eval_jaxpr/qkgd,ckd->kgqc/dot_general | solution.py:24
  58.3 2.0 fusion.56
  60.3 4.1 %fusion.57 = bf16[4,256,1,4,64]{1,4,3,2,0:T(8,128)(2,1)} fusion(bf16[4,256,1,4,64]{1,4,3,2,0:T(8,128)(2,1)} %get-tuple-element.258, s32[]{:T(128)S(6)} %copy.40, f32[2304,256,4]{1,0,2:T(8,128)S(1)} %get-tuple-element.241, f32[4,256]{1,0:T(4,128)S(1)} %get-tuple-element.242, pred[256,2304]{0,1:T(8,128)(4,1)S(1)} %compare_and_fusion.2, ...), kind=kOutput, calls=%fused_computation.12.clone.1 | convolution fusion | flops 311558144 | bytes 10461196 | tf_op jit(solution)/shard_map/while/body/eval_jaxpr/kgqc,ckd->kgqd/dot_general | solution.py:37
  64.4 0.6 dynamic_slice.80
  65.6 0.8 add_maximum_fusion.2
  66.4 1.1 compare_and_fusion.2
  67.5 2.6 %fusion.55 = (f32[4,256]{1,0:T(4,128)S(1)}, f32[2304,256,4]{1,0,2:T(8,128)S(1)}) fusion(pred[256,2304]{0,1:T(8,128)(4,1)S(1)} %compare_and_fusion.2, bf16[1024,1,4,64]{0,3,2,1:T(8,128)(2,1)} %get-tuple-element.277, s32[]{:T(128)S(6)} %select_n.82, bf16[3072,1,2,64]{0,3,2,1:T(8,128)(2,1)} %get-tuple-element.276, s32[]{:T(128)S(6)} %select_n.83), kind=kOutput, calls=%fused_computation.4.clone.1 | convolution fusion | flops 309066752 | bytes 10457096 | tf_op jit(solution)/shard_map/while/body/eval_jaxpr/qkgd,ckd->kgqc/dot_general | solution.py:24
  70.1 2.0 fusion.56
  72.1 4.1 %fusion.57 = bf16[4,256,1,4,64]{1,4,3,2,0:T(8,128)(2,1)} fusion(bf16[4,256,1,4,64]{1,4,3,2,0:T(8,128)(2,1)} %get-tuple-element.258, s32[]{:T(128)S(6)} %copy.40, f32[2304,256,4]{1,0,2:T(8,128)S(1)} %get-tuple-element.241, f32[4,256]{1,0:T(4,128)S(1)} %get-tuple-element.242, pred[256,2304]{0,1:T(8,128)(4,1)S(1)} %compare_and_fusion.2, ...), kind=kOutput, calls=%fused_computation.12.clone.1 | convolution fusion | flops 311558144 | bytes 10461196 | tf_op jit(solution)/shard_map/while/body/eval_jaxpr/kgqc,ckd->kgqd/dot_general | solution.py:37
  76.2 1.4 copy.29
  77.6 0.1 copy.36
  77.7 3.3 %convolution_convert_fusion = bf16[1024,2048]{1,0:T(8,128)(2,1)} fusion(bf16[1024,256]{0,1:T(8,128)(2,1)S(1)} %bitcast.93, bf16[256,2048]{1,0:T(8,128)(2,1)S(1)} %copy-done.1), kind=kOutput, calls=%fused_computation.25 | convolution fusion | flops 1075838976 | bytes 5767168 | tf_op jit(solution)/shard_map/dot_general | solution.py:122
  81.2 0.2 copy.33
  81.4 0.2 reshape.132
  81.6 1.7 select_reduce_fusion
  83.3 0.2 add_reduce_fusion
  83.5 0.2 convolution_convert_fusion.3
  83.7 0.8 reshape.133
  84.6 8.0 %all-to-all-start = ((bf16[32,4,1024]{2,1,0:T(4,128)(2,1)}), bf16[32,4,1024]{2,1,0:T(4,128)(2,1)S(1)}, u32[]{:S(2)}, u32[]{:S(2)}) async-start(bf16[32,4,1024]{2,1,0:T(4,128)(2,1)} %reshape.133), calls=%async_computation | async-start | bytes 524288 | tf_op jit(solution)/shard_map/all_to_all | solution.py:81
  92.8 8.5 %all-to-all-done = bf16[32,4,1024]{2,1,0:T(4,128)(2,1)S(1)} async-done(((bf16[32,4,1024]{2,1,0:T(4,128)(2,1)}), bf16[32,4,1024]{2,1,0:T(4,128)(2,1)S(1)}, u32[]{:S(2)}, u32[]{:S(2)}) %all-to-all-start) | async-done | bytes 262176 | tf_op jit(solution)/shard_map/all_to_all | solution.py:81
  101.4 0.7 convolution_convert_fusion.2
  102.1 0.3 reshape.135
  102.5 0.9 copy.34
  103.4 101.8 %all-reduce.2.cloned.1.call-done = bf16[1024,2048]{1,0:T(8,128)(2,1)} async-done(((bf16[1024,2048]{1,0:T(8,128)(2,1)}), bf16[1024,2048]{1,0:T(8,128)(2,1)}) %all-reduce.2.cloned.1.call-update) | async-done | bytes 4194320 | tf_op jit(solution)/shard_map/psum | solution.py:123
  205.2 1.9 convert_convert_fusion
  (25 shorter events, 0.5 us)
Async XLA Ops:
  7.2 1.6 copy-start
  7.2 198.0 %all-reduce.2.cloned.1.call-start = ((), (), s32[]{:S(2)}) async-start(), calls=%async_computation.1 | async-start | bytes 8388608 | tf_op jit(solution)/shard_map/psum | solution.py:123
  12.5 11.3 %collective-permute-start.1 = (bf16[1024,128]{0,1:T(8,128)(2,1)S(1)}, bf16[1024,128]{0,1:T(8,128)(2,1)S(1)}, u32[]{:S(2)}, u32[]{:S(2)}) collective-permute-start(bf16[1024,128]{0,1:T(8,128)(2,1)S(1)} %bitcast.95), channel_id=1, source_target_pairs={{0,8},{8,16},{16,24},{24,32},{32,40},{40,48},{48,56},{56,64},{64,7... | collective-permute-start | bytes 786440 | tf_op jit(solution)/shard_map/ppermute | solution.py:17
  16.1 12.1 %collective-permute-start = (bf16[1024,128]{0,1:T(8,128)(2,1)S(1)}, bf16[1024,128]{0,1:T(8,128)(2,1)S(1)}, u32[]{:S(2)}, u32[]{:S(2)}) collective-permute-start(bf16[1024,128]{0,1:T(8,128)(2,1)S(1)} %bitcast.96), channel_id=1, source_target_pairs={{0,16},{8,24},{16,32},{24,40},{32,48},{40,56},{48,64},{56,72},{64,... | collective-permute-start | bytes 786440 | tf_op jit(solution)/shard_map/ppermute | solution.py:17
  29.1 48.6 %copy-start.1 = (bf16[256,2048]{1,0:T(8,128)(2,1)S(1)}, bf16[256,2048]{1,0:T(8,128)(2,1)}, u32[]{:S(2)}) copy-start(bf16[256,2048]{1,0:T(8,128)(2,1)} %param.12) | copy-start | bytes 3145732
  77.7 3.3 %copy-start.2 = (s32[2048]{0:T(1024)S(1)}, s32[2048]{0:T(1024)}, u32[]{:S(2)}) copy-start(s32[2048]{0:T(1024)} %param.14) | copy-start | bytes 24580
  81.0 20.4 %copy-start.3 = (s32[2048]{0:T(1024)S(1)}, s32[2048]{0:T(1024)}, u32[]{:S(2)}) copy-start(s32[2048]{0:T(1024)} %param.15) | copy-start | bytes 24580
  84.6 16.8 %all-to-all-start = ((bf16[32,4,1024]{2,1,0:T(4,128)(2,1)}), bf16[32,4,1024]{2,1,0:T(4,128)(2,1)S(1)}, u32[]{:S(2)}, u32[]{:S(2)}) async-start(bf16[32,4,1024]{2,1,0:T(4,128)(2,1)} %reshape.133), calls=%async_computation | async-start | bytes 524288 | tf_op jit(solution)/shard_map/all_to_all | solution.py:81
Sparse Core Ops, SparseCore 0:
  81.2 124.0 all-reduce.1
where the time goes:
time: 215 us; the launch traced here: 214 us
  waiting for transfers between devices  115 us (53%)
  matrix products  39.2 us (18%)
  other arithmetic  20.2 us (9%)
  starting transfers between devices  14.7 us (7%)
  between operations  14.2 us (7%)
  local copies, waits for them, and re-layouts  8.25 us (4%)
  loops' own time  2.64 us (1%)
    psum x1, waiting for transfers between devices, body(): summed = lax.psum(projected.astype(jnp.bfloat16), 'tp').astype(jnp.float32)  102 us
    dot_general x4, matrix products, attend_band(): jnp.einsum('kgqc,ckd->kgqd', weights, values_block, preferred_element_typ...  16.3 us
    dot_general x4, matrix products, attend_band(): jnp.einsum('qkgd,ckd->kgqc', query_block, keys_block, preferred_element_t...  10.4 us
    all_to_all x1, waiting for transfers between devices, body(): lax.all_to_all(outgoing_pages, 'seq', split_axis=0, concat_axis=0, tiled=...  8.51 us
    all_to_all x1, starting transfers between devices, body(): lax.all_to_all(outgoing_pages, 'seq', split_axis=0, concat_axis=0, tiled=...  8.02 us
    reduce_sum x4, other arithmetic, attend_band(): row_total = jnp.sum(powered, axis=-1, keepdims=True)  7.98 us
    ppermute x2, starting transfers between devices, passed_along(): lax.ppermute(value, axis, [(source, source + steps) for source in range(l...  6.68 us
    dot_general x1, matrix products, body(): jnp.dot(tokens, w_query, preferred_element_type=jnp.float32)  4.58 us
  transfers between devices with their start and end apart: 4, of which 3 were waited for; matrix products, arithmetic and copies ran while one was open for 5% of the time, Pallas kernels for 0%

commit v1 on v0

--- a/solution.py
+++ b/solution.py
@@ -120,7 +120,9 @@
     attended = lax.map(one_block, jnp.arange(tok_rows // block_rows, dtype=jnp.int32))
     attended = attended.reshape(tok_rows, heads_dev * HD)
     projected = jnp.dot(attended, w_out, preferred_element_type=jnp.float32)
-    summed = lax.psum(projected.astype(jnp.bfloat16), "tp").astype(jnp.float32)
+    summed = jnp.sum(lax.all_gather(projected.astype(jnp.bfloat16), "tp"), axis=0).astype(
+        jnp.float32
+    )
     width_dev = summed.shape[1] // tp_count
     layer_out = lax.dynamic_slice_in_dim(summed, tp_index * width_dev, width_dev, 1).astype(
         jnp.bfloat16

time: 215 us -> 395 us (1.84); the launches traced: 214 us -> 388 us
  waiting for transfers between devices: 115 us -> 287 us
  other arithmetic: 20.2 us -> 33.6 us
  matrix products: 39.2 us -> 27.9 us
    all_gather x0 -> x1, waiting for transfers between devices: none -> 273 us  [body(): lax.all_gather(projected.astype(jnp.bfloat16), 'tp')]
    psum x1 -> x0, waiting for transfers between devices: 102 us -> none  [body(): summed = lax.psum(projected.astype(jnp.bfloat16), 'tp').astype(jnp.float32)]
    reduce_sum x0 -> x1, other arithmetic: none -> 14.3 us  [body(): jnp.sum(lax.all_gather(projected.astype(jnp.bfloat16), 'tp'), axis=0)]
    dot_general x4, matrix products: 16.3 us -> 9.47 us  [attend_band(): jnp.einsum('kgqc,ckd->kgqd', weights, values_block, preferred_element_typ...]
  transfers between devices with their start and end apart: 4 -> 4, of which waited for: 3 -> 3; matrix products, arithmetic and copies ran while one was open for 5% -> 2% of each run, Pallas kernels for 0% -> 0%
where the time goes in v1:
time: 395 us; the launch traced here: 388 us
  waiting for transfers between devices  287 us (73%)
  other arithmetic  33.6 us (9%)
  matrix products  27.9 us (7%)
  starting transfers between devices  14.7 us (4%)
  between operations  14.3 us (4%)
  local copies, waits for them, and re-layouts  7.49 us (2%)
    all_gather x1, waiting for transfers between devices, body(): lax.all_gather(projected.astype(jnp.bfloat16), 'tp')  273 us
    reduce_sum x1, other arithmetic, body(): jnp.sum(lax.all_gather(projected.astype(jnp.bfloat16), 'tp'), axis=0)  14.3 us
    dot_general x4, matrix products, attend_band(): jnp.einsum('kgqc,ckd->kgqd', weights, values_block, preferred_element_typ...  9.47 us
    all_to_all x1, waiting for transfers between devices, body(): lax.all_to_all(outgoing_pages, 'seq', split_axis=0, concat_axis=0, tiled=...  8.5 us
    reduce_sum x4, other arithmetic, attend_band(): row_total = jnp.sum(powered, axis=-1, keepdims=True)  8.04 us
    all_to_all x1, starting transfers between devices, body(): lax.all_to_all(outgoing_pages, 'seq', split_axis=0, concat_axis=0, tiled=...  8.02 us
  transfers between devices with their start and end apart: 4, of which 3 were waited for; matrix products, arithmetic and copies ran while one was open for 2% of the time, Pallas kernels for 0%

profile of v1, /device:TPU:65, one launch (start us, length us, event | category | flops | bytes accessed | tf_op | source)
XLA Modules:
  0.0 387.6 jit_solution(18393237024506932194)
XLA Ops:
  7.2 1.5 copy-done
  8.8 3.7 convolution_convert_fusion.4
  12.5 3.6 collective-permute-start.1
  16.1 3.1 collective-permute-start
  19.2 3.8 convolution_convert_fusion.1
  23.0 5.1 %collective-permute-done = bf16[1024,128]{0,1:T(8,128)(2,1)S(1)} collective-permute-done((bf16[1024,128]{0,1:T(8,128)(2,1)S(1)}, bf16[1024,128]{0,1:T(8,128)(2,1)S(1)}, u32[]{:S(2)}, u32[]{:S(2)}) %collective-permute-start) | collective-permute-done | bytes 262176 | tf_op jit(solution)/shard_map/ppermute | solution.py:17
  28.2 37.1 %while.15 = (s32[]{:T(128)}, bf16[4,256,1,4,64]{1,4,3,2,0:T(8,128)(2,1)S(1)}, s32[4]{0:T(128)S(1)}, s32[]{:T(128)}, s32[1024]{0:T(1024)}, /*index=5*/bf16[3072,1...) while((s32[]{:T(128)}, ...), condition=%wide.region_3.4_spmd, body=%wide.region_0.0_spmd.sunk | while | flops 631833600 | bytes 31567140 | solution.py:120
  28.2 0.7 dynamic_slice.80
  29.6 0.8 add_maximum_fusion.2
  30.4 1.1 compare_and_fusion.2
  31.5 1.7 fusion.55
  33.1 2.0 fusion.56
  35.1 2.4 fusion.57
  37.5 0.7 dynamic_slice.80
  38.9 0.8 add_maximum_fusion.2
  39.7 1.1 compare_and_fusion.2
  40.8 1.7 fusion.55
  42.4 2.0 fusion.56
  44.4 2.4 fusion.57
  46.8 0.7 dynamic_slice.80
  48.2 0.8 add_maximum_fusion.2
  49.0 1.1 compare_and_fusion.2
  50.0 1.7 fusion.55
  51.7 2.0 fusion.56
  53.7 2.4 fusion.57
  56.1 0.7 dynamic_slice.80
  57.5 0.8 add_maximum_fusion.2
  58.2 1.1 compare_and_fusion.2
  59.3 1.7 fusion.55
  61.0 2.0 fusion.56
  63.0 2.4 fusion.57
  65.4 0.4 copy.29
  65.8 0.1 copy.36
  65.9 3.3 convolution_convert_fusion
  69.5 0.2 copy.33
  69.6 0.2 reshape.132
  69.9 1.7 select_reduce_fusion
  71.6 0.2 add_reduce_fusion
  71.7 0.2 convolution_convert_fusion.3
  72.0 0.8 reshape.133
  72.8 8.0 %all-to-all-start = ((bf16[32,4,1024]{2,1,0:T(4,128)(2,1)}), bf16[32,4,1024]{2,1,0:T(4,128)(2,1)S(1)}, u32[]{:S(2)}, u32[]{:S(2)}) async-start(bf16[32,4,1024]{2,1,0:T(4,128)(2,1)} %reshape.133), calls=%async_computation | async-start | bytes 524288 | tf_op jit(solution)/shard_map/all_to_all | solution.py:81
  81.0 8.5 %all-to-all-done = bf16[32,4,1024]{2,1,0:T(4,128)(2,1)S(1)} async-done(((bf16[32,4,1024]{2,1,0:T(4,128)(2,1)}), bf16[32,4,1024]{2,1,0:T(4,128)(2,1)S(1)}, u32[]{:S(2)}, u32[]{:S(2)}) %all-to-all-start) | async-done | bytes 262176 | tf_op jit(solution)/shard_map/all_to_all | solution.py:81
  89.6 0.7 convolution_convert_fusion.2
  90.4 0.3 reshape.135
  90.7 0.9 copy.34
  91.6 273.0 %all-gather.3.cloned.1.call-done = bf16[8192,2048]{1,0:T(8,128)(2,1)} async-done(((bf16[1024,2048]{1,0:T(8,128)(2,1)}), bf16[8192,2048]{1,0:T(8,128)(2,1)}) %all-gather.3.cloned.1.call-update) | async-done | bytes 33554448 | tf_op jit(solution)/shard_map/all_gather | solution.py:123
  364.6 14.3 %reduce_sum.30 = bf16[1024,2048]{1,0:T(8,128)(2,1)} reduce(bf16[8,1024,2048]{2,1,0:T(8,128)(2,1)} %bitcast.94, bf16[]{:T(256)} %constant.147.clone.1), dimensions={0}, to_apply=%region_4.5 | reduce | flops 14680064 | bytes 37748736 | tf_op jit(solution)/shard_map/reduce_sum | solution.py:123
  378.9 1.9 convert_convert_fusion
  (28 shorter events, 0.6 us)
Async XLA Ops:
  7.2 1.6 copy-start
  7.2 357.4 %all-gather.3.cloned.1.call-start = ((), (), s32[]{:S(2)}) async-start(), calls=%async_computation.1 | async-start | bytes 37748736 | tf_op jit(solution)/shard_map/all_gather | solution.py:123
  12.5 10.5 %collective-permute-start.1 = (bf16[1024,128]{0,1:T(8,128)(2,1)S(1)}, bf16[1024,128]{0,1:T(8,128)(2,1)S(1)}, u32[]{:S(2)}, u32[]{:S(2)}) collective-permute-start(bf16[1024,128]{0,1:T(8,128)(2,1)S(1)} %bitcast.97), channel_id=1, source_target_pairs={{0,8},{8,16},{16,24},{24,32},{32,40},{40,48},{48,56},{56,64},{64,7... | collective-permute-start | bytes 786440 | tf_op jit(solution)/shard_map/ppermute | solution.py:17
  16.1 12.1 %collective-permute-start = (bf16[1024,128]{0,1:T(8,128)(2,1)S(1)}, bf16[1024,128]{0,1:T(8,128)(2,1)S(1)}, u32[]{:S(2)}, u32[]{:S(2)}) collective-permute-start(bf16[1024,128]{0,1:T(8,128)(2,1)S(1)} %bitcast.98), channel_id=1, source_target_pairs={{0,16},{8,24},{16,32},{24,40},{32,48},{40,56},{48,64},{56,72},{64,... | collective-permute-start | bytes 786440 | tf_op jit(solution)/shard_map/ppermute | solution.py:17
  28.2 37.7 %copy-start.2 = (bf16[256,2048]{1,0:T(8,128)(2,1)S(1)}, bf16[256,2048]{1,0:T(8,128)(2,1)}, u32[]{:S(2)}) copy-start(bf16[256,2048]{1,0:T(8,128)(2,1)} %param.12) | copy-start | bytes 3145732
  65.9 3.4 copy-start.3
  69.2 20.4 %copy-start.4 = (s32[2048]{0:T(1024)S(1)}, s32[2048]{0:T(1024)}, u32[]{:S(2)}) copy-start(s32[2048]{0:T(1024)} %param.15) | copy-start | bytes 24580
  72.8 16.8 %all-to-all-start = ((bf16[32,4,1024]{2,1,0:T(4,128)(2,1)}), bf16[32,4,1024]{2,1,0:T(4,128)(2,1)S(1)}, u32[]{:S(2)}, u32[]{:S(2)}) async-start(bf16[32,4,1024]{2,1,0:T(4,128)(2,1)} %reshape.133), calls=%async_computation | async-start | bytes 524288 | tf_op jit(solution)/shard_map/all_to_all | solution.py:81
  364.6 16.2 %copy-start.1 = (bf16[2048,512]{1,0:T(8,128)(2,1)S(1)}, bf16[2048,512]{1,0:T(8,128)(2,1)}, u32[]{:S(2)}) copy-start(bf16[2048,512]{1,0:T(8,128)(2,1)} %param.11) | copy-start | bytes 6291460
Sparse Core Ops, SparseCore 0:
  69.4 295.1 all-gather.2
